TPU v7x, 32 devices: a whole 2x2x4 slice. The times are simulated.
32 devices in a mesh: groups: 2 (over y), expert: 4 (over z), dp: 4 (over x, core).
Axes of the slice: x: 2, y: 2, z: 4, core: 2. Of those that a mesh axis runs over, the one named last changes fastest.
Arguments:
- out_grad: bfloat16 [4096, 2048], P(('groups', 'expert', 'dp')), parts along dimension 0, may hold values from -0.5 to 0.5
- gate_weights: bfloat16 [4096, 8], P(('groups', 'expert', 'dp')), parts along dimension 0, may hold values from 0.049804688 to 0.5
- expert_ids: int32 [4096, 8], P(('groups', 'expert', 'dp')), parts along dimension 0, may hold values from 0 to 31, all different within a row; in each aligned block of 128 rows (0 to 127, 128 to 255, ...) at most 36 rows name the same one
- hidden: bfloat16 [32, 8, 4, 36, 768], P('expert', ('groups', 'dp')), parts along dimension 1, may hold values from -6 to 6
- down_weight: bfloat16 [32, 768, 2048], P('expert', None, 'dp'), may hold values from -0.21875 to 0.21875
Outputs:
- weight_grad: float32 [64, 768, 2048], P(('groups', 'expert'), None, 'dp'), parts along dimension 0
- gate_grad: float32 [4096, 8], P(('groups', 'expert', 'dp')), parts along dimension 0
There are 2 independent parts, one for each index of `groups`. A program takes and returns all parts, laid end to end along the dimension named above; an argument that names none is the same for every part. Nothing has to cross between parts.
Inputs may be any that keep to these rules, and one draw needn't show every extreme that they name: `expert_ids`: each token names 8 different experts; within each block of 128 tokens (one device's tokens) no expert is named by more than 36 tokens, a bound that some block reaches.
All inputs are finite; a program needn't handle non-finite values.
Results may differ from a plain program's by a relative error of at most 0.0095.
Values may be sent and summed in bfloat16 or wider, within the bound.
No kernel may reach another device: no remote copies, remote signals or barrier semaphores. Data moves between devices by JAX's collectives and lax.ppermute only.
A program may use at most 128 MiB of HBM per device.

v0:
```python
import jax
import jax.numpy as jnp
from jax import lax
from jax.sharding import PartitionSpec as P


def per_device(out_grad, gate_weights, expert_ids, hidden, down_weight):
    tok_rows, top_count = expert_ids.shape
    row_width = out_grad.shape[1]
    local_count = hidden.shape[0]
    source_count = hidden.shape[2]
    capacity = hidden.shape[3]
    hidden_width = hidden.shape[4]
    peer_count = lax.axis_size("expert")
    shards = lax.axis_size("dp")
    expert_count = local_count * peer_count
    col_width = row_width // shards
    block_count = peer_count * shards
    f32 = jnp.float32
    bf16 = jnp.bfloat16
    cols = out_grad.reshape(tok_rows, shards, col_width)
    cols = lax.all_to_all(cols, "dp", split_axis=1, concat_axis=0, tiled=True)
    cols = cols.reshape(shards, tok_rows, col_width)
    grad_all = lax.all_gather(cols, "expert", axis=0, tiled=False)
    grad_all = grad_all.reshape(block_count, tok_rows, col_width)
    ids_all = lax.all_gather(expert_ids, ("expert", "dp"), axis=0, tiled=True)
    ids_all = ids_all.reshape(block_count, tok_rows, top_count)
    gate_all = lax.all_gather(gate_weights, ("expert", "dp"), axis=0, tiled=True)
    gate_all = gate_all.reshape(block_count, tok_rows, top_count)
    hidden_all = lax.all_gather(hidden, "dp", axis=1, tiled=True)
    my_experts = lax.axis_index("expert") * local_count + jnp.arange(local_count, dtype=jnp.int32)
    hit = ids_all[:, :, :, None] == my_experts[None, None, None, :]
    chose = jnp.any(hit, axis=2)
    gate_hit = jnp.sum(jnp.where(hit, gate_all.astype(f32)[:, :, :, None], 0.0), axis=2)
    before = (jnp.arange(tok_rows)[:, None] < jnp.arange(tok_rows)[None, :]).astype(bf16)
    rank = jnp.einsum("bul,ut->btl", chose.astype(bf16), before, preferred_element_type=f32).astype(
        jnp.int32
    )
    slot_ids = jnp.arange(capacity, dtype=jnp.int32)
    chose_t = chose.transpose(0, 2, 1)
    rank_t = rank.transpose(0, 2, 1)
    gate_t = gate_hit.transpose(0, 2, 1)
    select = chose_t[:, :, None, :] & (rank_t[:, :, None, :] == slot_ids[None, None, :, None])
    select_gate = jnp.where(select, gate_t[:, :, None, :], 0.0).astype(bf16)
    grad_rows = jnp.einsum(
        "blct,btd->blcd", select.astype(bf16), grad_all, preferred_element_type=f32
    ).astype(bf16)
    scaled = jnp.einsum("blct,btd->blcd", select_gate, grad_all, preferred_element_type=f32).astype(
        bf16
    )
    grad_rows = grad_rows.reshape(peer_count, shards, local_count, capacity, col_width)
    scaled = scaled.reshape(peer_count, shards, local_count, capacity, col_width)
    weight_grad = None
    for replica in range(shards):
        part = (
            jnp.einsum(
                "lscf,slcd->lfd",
                hidden_all[:, replica],
                scaled[:, replica],
                preferred_element_type=f32,
            )
            .astype(bf16)
            .astype(f32)
        )
        weight_grad = part if weight_grad is None else weight_grad + part
    expert_out = jnp.einsum("liscf,lfd->silcd", hidden_all, down_weight, preferred_element_type=f32)
    slot_part = jnp.sum(grad_rows.astype(f32) * expert_out, axis=4)
    send_back = slot_part.reshape(block_count, local_count, capacity)
    returned = lax.all_to_all(send_back, ("expert", "dp"), split_axis=0, concat_axis=0, tiled=True)
    returned = returned.reshape(peer_count, shards, local_count, capacity)
    slot_grad = jnp.sum(returned, axis=1).reshape(expert_count * capacity)
    own_chose = jnp.any(
        expert_ids[:, :, None] == jnp.arange(expert_count, dtype=jnp.int32)[None, None, :], axis=1
    )
    own_rank = jnp.einsum(
        "ue,ut->te", own_chose.astype(bf16), before, preferred_element_type=f32
    ).astype(jnp.int32)
    own_slot = jnp.take_along_axis(own_rank, expert_ids, axis=1)
    gate_grad = slot_grad[expert_ids * capacity + own_slot]
    return (weight_grad, gate_grad)


def solution(mesh):
    return jax.shard_map(
        per_device,
        mesh=mesh,
        in_specs=(
            P(("groups", "expert", "dp"), None),
            P(("groups", "expert", "dp"), None),
            P(("groups", "expert", "dp"), None),
            P("expert", ("groups", "dp"), None, None, None),
            P("expert", None, "dp"),
        ),
        out_specs=(P(("groups", "expert"), None, "dp"), P(("groups", "expert", "dp"), None)),
        check_vma=False,
    )
```

profile of v0, /device:TPU:0, one launch (start us, length us, event | category | flops | bytes accessed | tf_op | source)
XLA Modules:
  0.0 189.4 jit_solution(14676324695385926704)
XLA Ops:
  7.2 1.4 copy.113
  8.7 12.9 %all_to_all.20 = bf16[128,4,512]{0,2,1:T(8,128)(2,1)S(1)} all-to-all(bf16[128,4,512]{0,2,1:T(8,128)(2,1)S(1)} %bitcast.95), channel_id=1, replica_groups=mesh['groups'=2,'expert'=4,'dp'=4] {'dp'}, dimensions={1} | all-to-all | bytes 1048576 | tf_op jit(solution)/shard_map/all_to_all | solution.py:22
  21.5 1.0 copy.114
  22.6 1.8 copy.116
  24.5 0.1 copy.127
  24.7 0.1 convolution_convert_fusion.3
  24.8 7.0 %gather_fusion.1 = s32[1024]{0:T(1024)S(1)} fusion(s32[128,32]{0,1:T(8,128)S(1)} %convolution_convert_fusion.3, s32[1024]{0:T(1024)S(1)} %reshape.69), kind=kCustom, calls=%fused_computation.1 | custom fusion | bytes 16384 | tf_op jit(solution)/shard_map/jit(take_along_axis)/gather | solution.py:78
  32.0 0.1 copy.129
  32.2 21.2 %all_gather.13 = bf16[2048,8]{0,1:T(8,128)(2,1)S(1)} all-gather(bf16[128,8]{0,1:T(8,128)(2,1)S(1)} %copy-done.5), channel_id=1, replica_groups=mesh['groups'=2,'expert'=4,'dp'=4] {'expert','dp'}, dimensions={0}, use_global_device_ids=true | all-gather | bytes 34816 | tf_op jit(solution)/shard_map/all_gather | solution.py:28
  53.4 18.1 %all_gather.12 = s32[2048,8]{0,1:T(8,128)S(1)} all-gather(s32[128,8]{0,1:T(8,128)S(1)} %copy-done.4), channel_id=1, replica_groups=mesh['groups'=2,'expert'=4,'dp'=4] {'expert','dp'}, dimensions={0}, use_global_device_ids=true | all-gather | bytes 69632 | tf_op jit(solution)/shard_map/all_gather | solution.py:26
  71.5 0.1 compare_reduce_fusion
  71.7 0.1 fusion.21
  71.8 0.1 convolution_convert_fusion.2
  72.0 3.1 %convolution_convert_fusion = bf16[16,8,36,512]{3,2,1,0:T(8,128)(2,1)S(1)} fusion(bf16[16,128,1,512]{3,1,2,0:T(8,128)(2,1)} %all-gather.6.cloned.1.call-done, bf16[16,8,128]{2,1,0:T(8,128)(2,1)S(1)} %bitcast.101, s32[16,8,128]{2,1,0:T(8,128)S(1)} %convolution_convert_fusion.2, pred[16,8,128]{2,1,0:T(8,128)(4,1)S(1)} %bitcast.98), kind=kOutput, calls=%fused_computation.12 | convolution fusion | flops 608108544 | bytes 6930432 | tf_op jit(solution)/shard_map/blct,btd->blcd/dot_general | solution.py:48
  75.1 2.0 %fusion.27 = (bf16[4,1,8,36,512]{4,3,2,1,0:T(8,128)(2,1)S(1)}, bf16[4,1,8,36,512]{4,3,2,1,0:T(8,128)(2,1)}, bf16[4,1,8,36,512]{4,3,2,1,0:T(8,128)(2,1)}, bf16[4,1,8,36,512]{4,3,2,1,0:T(8,128)(2,1)S(1)}) fusion(bf16[4,4,8,36,512]{4,3,2,1,0:T(8,128)(2,1)S(1)} %bitcast.93), kind=kLoop, calls=%fused_computation.55 | loop fusion | bytes 9437184 | tf_op jit(solution)/shard_map/slice | solution.py:59
  77.1 0.5 copy-done
  77.6 6.0 %bitcast_convert_fusion.5 = f32[4,4,8,36,512]{4,3,2,1,0:T(8,128)} fusion(bf16[16,128,1,512]{3,1,2,0:T(8,128)(2,1)S(1)} %copy-done, s32[16,8,128]{2,1,0:T(8,128)S(1)} %convolution_convert_fusion.2, pred[16,8,128]{2,1,0:T(8,128)(4,1)S(1)} %bitcast.99), kind=kOutput, calls=%fused_computation.52 | convolution fusion | flops 609878016 | bytes 11616256 | tf_op jit(solution)/shard_map/blct,btd->blcd/dot_general | solution.py:45
  83.7 37.0 %all-gather.4.cloned.1.call-done = bf16[8,4,4,36,768]{4,0,3,2,1:T(8,128)(2,1)} async-done(((bf16[8,1,4,36,768]{4,0,3,2,1:T(8,128)(2,1)}), bf16[8,4,4,36,768]{4,0,3,2,1:T(8,128)(2,1)}) %all-gather.4.cloned.1.call-update) | async-done | bytes 7077904 | tf_op jit(solution)/shard_map/all_gather | solution.py:30
  120.7 11.1 %fusion = f32[4,4,8,36]{3,0,1,2:T(4,128)S(1)} fusion(f32[4,4,8,36,512]{4,3,2,1,0:T(8,128)} %bitcast_convert_fusion.5, bf16[8,4,4,36,768]{4,0,3,2,1:T(8,128)(2,1)} %all-gather.4.cloned.1.call-done, bf16[8,768,512]{2,1,0:T(8,128)(2,1)} %param.9), kind=kOutput, calls=%fused_computation.8 | convolution fusion | flops 3628592640 | bytes 22824960 | tf_op jit(solution)/shard_map/liscf,lfd->silcd/dot_general | solution.py:66
  131.8 0.7 reshape.91
  132.5 4.7 %all-to-all-start.1 = ((f32[16,1,288]{2,1,0:T(1,128)}), f32[16,1,288]{2,1,0:T(1,128)S(1)}, u32[]{:S(2)}, u32[]{:S(2)}) async-start(f32[16,1,288]{2,1,0:T(1,128)} %reshape.91), calls=%async_computation.1 | async-start | bytes 49152 | tf_op jit(solution)/shard_map/all_to_all | solution.py:69
  137.3 3.6 %fusion.26 = (bf16[8,1,4,36,768]{4,0,3,2,1:T(8,128)(2,1)S(1)}, bf16[8,1,4,36,768]{4,0,3,2,1:T(8,128)(2,1)S(1)}, bf16[8,1,4,36,768]{4,0,3,2,1:T(8,128)(2,1)S(1)}, bf16[8,1,4,36,768]{4,0,3,2,1:T(8,128)(2,1)S(1)}) fusion(bf16[8,4,4,36,768]{4,0,3,2,1:T(8,128)(2,1)} %all-gather.4.cloned.1.call-done), kind=kLoop, calls=%fused_computation.54 | loop fusion | bytes 14155776 | tf_op jit(solution)/shard_map/slice | solution.py:58
  140.9 2.0 %fusion.12 = bf16[8,512,768,1]{2,1,3,0:T(8,128)(2,1)S(1)} fusion(bf16[8,1,4,36,768]{4,0,3,2,1:T(8,128)(2,1)S(1)} %get-tuple-element.15, bf16[4,1,8,36,512]{4,3,2,1,0:T(8,128)(2,1)S(1)} %copy-done.3), kind=kOutput, calls=%fused_computation.21 | convolution fusion | flops 905969664 | bytes 9240576 | tf_op jit(solution)/shard_map/lscf,slcd->lfd/dot_general | solution.py:56
  143.0 4.7 %fusion.13 = bf16[8,512,768,1]{2,1,3,0:T(8,128)(2,1)} fusion(bf16[8,1,4,36,768]{4,0,3,2,1:T(8,128)(2,1)S(1)} %get-tuple-element.16, bf16[4,1,8,36,512]{4,3,2,1,0:T(8,128)(2,1)S(1)} %copy-done.2), kind=kOutput, calls=%fused_computation.23 | convolution fusion | flops 905969664 | bytes 9240576 | tf_op jit(solution)/shard_map/lscf,slcd->lfd/dot_general | solution.py:56
  147.6 4.8 %fusion.14 = bf16[8,512,768,1]{2,1,3,0:T(8,128)(2,1)} fusion(bf16[8,1,4,36,768]{4,0,3,2,1:T(8,128)(2,1)S(1)} %get-tuple-element.17, bf16[4,1,8,36,512]{4,3,2,1,0:T(8,128)(2,1)S(1)} %get-tuple-element.21), kind=kOutput, calls=%fused_computation.25 | convolution fusion | flops 905969664 | bytes 9240576 | tf_op jit(solution)/shard_map/lscf,slcd->lfd/dot_general | solution.py:56
  152.4 9.2 %add_bitcast_fusion = f32[8,768,512]{1,2,0:T(8,128)} fusion(bf16[8,512,768,1]{2,1,3,0:T(8,128)(2,1)} %fusion.14, bf16[8,512,768,1]{2,1,3,0:T(8,128)(2,1)} %fusion.13, bf16[8,512,768,1]{2,1,3,0:T(8,128)(2,1)S(1)} %fusion.12, bf16[8,1,4,36,768]{4,0,3,2,1:T(8,128)(2,1)S(1)} %get-tuple-element.14, bf16[4,1,8,36,512]{4,3,2,1,0:T(8,128)(2,1)S(1)} %get-tuple-element.18), kind=kOutput, calls=%fused_computation.6 | convolution fusion | flops 931135488 | bytes 34406400 | tf_op jit(solution)/shard_map/lscf,slcd->lfd/dot_general | solution.py:56
  161.6 12.6 %copy.130 = f32[8,768,512]{2,1,0:T(8,128)} copy(f32[8,768,512]{1,2,0:T(8,128)} %add_bitcast_fusion) | data formatting | bytes 25165824
  174.2 0.5 broadcast.36
  174.7 0.7 reduce
  175.6 0.1 reshape.57
  175.7 6.2 %gather_fusion = f32[1024]{0:T(1024)S(1)} fusion(f32[1152]{0:T(1024)S(1)} %reshape.57, s32[1024]{0:T(1024)S(1)} %broadcast_clamp_fusion), kind=kCustom, calls=%fused_computation | custom fusion | bytes 12288 | tf_op jit(solution)/shard_map/gather | solution.py:79
  181.9 0.7 copy.131
  (31 shorter events, 0.7 us)
Async XLA Ops:
  7.2 15.5 %copy-start.1 = (bf16[8,1,4,36,768]{4,2,3,1,0:T(4,128)(2,1)S(1)}, bf16[8,1,4,36,768]{4,2,3,1,0:T(4,128)(2,1)}, u32[]{:S(2)}) copy-start(bf16[8,1,4,36,768]{4,2,3,1,0:T(4,128)(2,1)} %param.8) | copy-start | bytes 5308420
  7.2 64.8 %all-gather.6.cloned.1.call-start = ((), (), s32[]{:S(2)}) async-start(), calls=%async_computation.3 | async-start | bytes 2621440 | tf_op jit(solution)/shard_map/all_gather | solution.py:24
  22.6 1.9 copy-start.4
  22.6 98.1 %all-gather.4.cloned.1.call-start = ((), (), s32[]{:S(2)}) async-start(), calls=%async_computation.2 | async-start | bytes 8847360 | tf_op jit(solution)/shard_map/all_gather | solution.py:30
  24.8 7.4 %copy-start.5 = (bf16[128,8]{0,1:T(8,128)(2,1)S(1)}, bf16[128,8]{0,1:T(8,128)(2,1)}, u32[]{:S(2)}) copy-start(bf16[128,8]{0,1:T(8,128)(2,1)} %param.6) | copy-start | bytes 6148
  75.1 2.5 %copy-start = (bf16[16,128,1,512]{3,1,2,0:T(8,128)(2,1)S(1)}, bf16[16,128,1,512]{3,1,2,0:T(8,128)(2,1)}, u32[]{:S(2)}) copy-start(bf16[16,128,1,512]{3,1,2,0:T(8,128)(2,1)} %all-gather.6.cloned.1.call-done) | copy-start | bytes 6291460
  132.5 41.7 %all-to-all-start.1 = ((f32[16,1,288]{2,1,0:T(1,128)}), f32[16,1,288]{2,1,0:T(1,128)S(1)}, u32[]{:S(2)}, u32[]{:S(2)}) async-start(f32[16,1,288]{2,1,0:T(1,128)} %reshape.91), calls=%async_computation.1 | async-start | bytes 49152 | tf_op jit(solution)/shard_map/all_to_all | solution.py:69
  137.3 3.6 %copy-start.3 = (bf16[4,1,8,36,512]{4,3,2,1,0:T(8,128)(2,1)S(1)}, bf16[4,1,8,36,512]{4,3,2,1,0:T(8,128)(2,1)}, u32[]{:S(2)}) copy-start(bf16[4,1,8,36,512]{4,3,2,1,0:T(8,128)(2,1)} %get-tuple-element.19) | copy-start | bytes 3538948
  140.9 2.1 %copy-start.2 = (bf16[4,1,8,36,512]{4,3,2,1,0:T(8,128)(2,1)S(1)}, bf16[4,1,8,36,512]{4,3,2,1,0:T(8,128)(2,1)}, u32[]{:S(2)}) copy-start(bf16[4,1,8,36,512]{4,3,2,1,0:T(8,128)(2,1)} %get-tuple-element.20) | copy-start | bytes 3538948
Sparse Core Ops, SparseCore 0:
  22.7 46.6 all-gather.5
  70.9 49.7 all-gather.3
where the time goes:
time: 190 us; the launch traced here: 189 us
  blocking collectives  52.1 us (27%)
  matrix products  41.3 us (22%)
  local copies, waits for them, and re-layouts  38.8 us (20%)
  waiting for transfers between devices  37.1 us (20%)
  between operations  14.3 us (8%)
  starting transfers between devices  4.8 us (3%)
    all_gather x1, waiting for transfers between devices, per_device(): hidden_all = lax.all_gather(hidden, 'dp', axis=1, tiled=True)  37 us
    all_gather x1, blocking collectives, per_device(): lax.all_gather(gate_weights, ('expert', 'dp'), axis=0, tiled=True)  21.2 us
    dot_general x4, matrix products, per_device(): jnp.einsum('lscf,slcd->lfd', hidden_all[:, replica], scaled[:, replica],...  20.7 us
    all_gather x1, blocking collectives, per_device(): ids_all = lax.all_gather(expert_ids, ('expert', 'dp'), axis=0, tiled=True)  18.1 us
    unnamed x18, local copies, waits for them, and re-layouts  17.8 us
    all_to_all x1, blocking collectives, per_device(): cols = lax.all_to_all(cols, 'dp', split_axis=1, concat_axis=0, tiled=True)  12.9 us
    dot_general x1, matrix products, per_device(): jnp.einsum('liscf,lfd->silcd', hidden_all, down_weight, preferred_element...  11.1 us
    gather x5, local copies, waits for them, and re-layouts, per_device(): own_slot = jnp.take_along_axis(own_rank, expert_ids, axis=1)  7.34 us
  transfers between devices with their start and end apart: 3, of which 1 were waited for; matrix products, arithmetic and copies ran while one was open for 31% of the time, Pallas kernels for 0%

commit v1 on v0

--- a/solution.py
+++ b/solution.py
@@ -25,7 +25,12 @@
     grad_all = grad_all.reshape(block_count, tok_rows, col_width)
     ids_all = lax.all_gather(expert_ids, ("expert", "dp"), axis=0, tiled=True)
     ids_all = ids_all.reshape(block_count, tok_rows, top_count)
-    gate_all = lax.all_gather(gate_weights, ("expert", "dp"), axis=0, tiled=True)
+    gate_all = jnp.concatenate(
+        lax.all_to_all(
+            jnp.stack([gate_weights] * lax.axis_size(("expert", "dp"))), ("expert", "dp"), 0, 0
+        ),
+        axis=0,
+    )
     gate_all = gate_all.reshape(block_count, tok_rows, top_count)
     hidden_all = lax.all_gather(hidden, "dp", axis=1, tiled=True)
     my_experts = lax.axis_index("expert") * local_count + jnp.arange(local_count, dtype=jnp.int32)

time: 190 us -> 190 us (level)
  blocking collectives: 52.1 us -> 35.4 us
  waiting for transfers between devices: 37.1 us -> 48.2 us
  starting transfers between devices: 4.8 us -> 9.78 us
    all_gather x1 -> x0, blocking collectives: 21.2 us -> none  [per_device(): lax.all_gather(gate_weights, ('expert', 'dp'), axis=0, tiled=True)]
    all_gather x1, waiting for transfers between devices: 0.02 us -> 8.91 us  [per_device(): grad_all = lax.all_gather(cols, 'expert', axis=0, tiled=False)]
    all_to_all x0 -> x1, starting transfers between devices: none -> 4.98 us  [per_device(): lax.all_to_all(jnp.stack([gate_weights] * lax.axis_size(('expert', 'dp'))...]
    all_gather x1, blocking collectives: 18.1 us -> 22.6 us  [per_device(): ids_all = lax.all_gather(expert_ids, ('expert', 'dp'), axis=0, tiled=True)]
    all_gather x1, waiting for transfers between devices: 37 us -> 39.2 us  [per_device(): hidden_all = lax.all_gather(hidden, 'dp', axis=1, tiled=True)]
  transfers between devices with their start and end apart: 3 -> 4, of which waited for: 1 -> 2; matrix products, arithmetic and copies ran while one was open for 31% -> 31% of each run, Pallas kernels for 0% -> 0%
where the time goes in v1:
time: 190 us
  waiting for transfers between devices  48.2 us (25%)
  matrix products  42.1 us (22%)
  local copies, waits for them, and re-layouts  39 us (21%)
  blocking collectives  35.4 us (19%)
  between operations  14.3 us (8%)
  starting transfers between devices  9.78 us (5%)
    all_gather x1, waiting for transfers between devices, per_device(): hidden_all = lax.all_gather(hidden, 'dp', axis=1, tiled=True)  39.2 us
    all_gather x1, blocking collectives, per_device(): ids_all = lax.all_gather(expert_ids, ('expert', 'dp'), axis=0, tiled=True)  22.6 us
    dot_general x4, matrix products, per_device(): jnp.einsum('lscf,slcd->lfd', hidden_all[:, replica], scaled[:, replica],...  20.7 us
    unnamed x18, local copies, waits for them, and re-layouts  17.3 us
    all_to_all x1, blocking collectives, per_device(): cols = lax.all_to_all(cols, 'dp', split_axis=1, concat_axis=0, tiled=True)  12.9 us
    dot_general x1, matrix products, per_device(): jnp.einsum('liscf,lfd->silcd', hidden_all, down_weight, preferred_element...  11.1 us
    all_gather x1, waiting for transfers between devices, per_device(): grad_all = lax.all_gather(cols, 'expert', axis=0, tiled=False)  8.91 us
    gather x5, local copies, waits for them, and re-layouts, per_device(): own_slot = jnp.take_along_axis(own_rank, expert_ids, axis=1)  7.34 us
  transfers between devices with their start and end apart: 4, of which 2 were waited for; matrix products, arithmetic and copies ran while one was open for 31% of the time, Pallas kernels for 0%

profile of v1, /device:TPU:0, one launch (start us, length us, event | category | flops | bytes accessed | tf_op | source)
XLA Modules:
  0.0 189.8 jit_solution(16271496279451681902)
XLA Ops:
  7.2 1.4 copy.113
  8.7 12.9 %all_to_all.25 = bf16[128,4,512]{0,2,1:T(8,128)(2,1)S(1)} all-to-all(bf16[128,4,512]{0,2,1:T(8,128)(2,1)S(1)} %bitcast.92), channel_id=1, replica_groups=mesh['groups'=2,'expert'=4,'dp'=4] {'dp'}, dimensions={1} | all-to-all | bytes 1048576 | tf_op jit(solution)/shard_map/all_to_all | solution.py:22
  21.5 1.0 copy.114
  22.7 1.8 copy.116
  24.5 0.6 stack.2
  25.1 5.0 %all-to-all-start = ((bf16[16,128,8]{1,2,0:T(8,128)(2,1)}), bf16[16,128,8]{1,2,0:T(8,128)(2,1)S(1)}, u32[]{:S(2)}, u32[]{:S(2)}) async-start(bf16[16,128,8]{1,2,0:T(8,128)(2,1)} %stack.2), calls=%async_computation | async-start | bytes 65536 | tf_op jit(solution)/shard_map/all_to_all | solution.py:29
  30.1 0.1 copy.127
  30.3 0.1 convolution_convert_fusion.3
  30.4 7.0 %gather_fusion.1 = s32[1024]{0:T(1024)S(1)} fusion(s32[128,32]{0,1:T(8,128)S(1)} %convolution_convert_fusion.3, s32[1024]{0:T(1024)S(1)} %reshape.63), kind=kCustom, calls=%fused_computation.1 | custom fusion | bytes 16384 | tf_op jit(solution)/shard_map/jit(take_along_axis)/gather | solution.py:83
  37.6 0.1 copy.129
  37.8 22.6 %all_gather.9 = s32[2048,8]{0,1:T(8,128)S(1)} all-gather(s32[128,8]{0,1:T(8,128)S(1)} %copy-done.4), channel_id=1, replica_groups=mesh['groups'=2,'expert'=4,'dp'=4] {'expert','dp'}, dimensions={0}, use_global_device_ids=true | all-gather | bytes 69632 | tf_op jit(solution)/shard_map/all_gather | solution.py:26
  60.4 0.1 compare_reduce_fusion
  60.6 0.1 convolution_convert_fusion.2
  60.7 0.1 fusion.21
  60.9 8.9 %all-gather.6.cloned.1.call-done = bf16[16,128,1,512]{3,1,2,0:T(8,128)(2,1)} async-done(((bf16[4,128,1,512]{3,1,2,0:T(8,128)(2,1)}), bf16[16,128,1,512]{3,1,2,0:T(8,128)(2,1)}) %all-gather.6.cloned.1.call-update) | async-done | bytes 2097168 | tf_op jit(solution)/shard_map/all_gather | solution.py:24
  69.8 3.1 %convolution_convert_fusion = bf16[16,8,36,512]{3,2,1,0:T(8,128)(2,1)S(1)} fusion(bf16[16,128,1,512]{3,1,2,0:T(8,128)(2,1)} %all-gather.6.cloned.1.call-done, bf16[16,8,128]{2,1,0:T(8,128)(2,1)S(1)} %bitcast.98, s32[16,8,128]{2,1,0:T(8,128)S(1)} %convolution_convert_fusion.2, pred[16,8,128]{2,1,0:T(8,128)(4,1)S(1)} %bitcast.95), kind=kOutput, calls=%fused_computation.12 | convolution fusion | flops 608108544 | bytes 6930432 | tf_op jit(solution)/shard_map/blct,btd->blcd/dot_general | solution.py:53
  72.9 2.0 %fusion.27 = (bf16[4,1,8,36,512]{4,3,2,1,0:T(8,128)(2,1)S(1)}, bf16[4,1,8,36,512]{4,3,2,1,0:T(8,128)(2,1)}, bf16[4,1,8,36,512]{4,3,2,1,0:T(8,128)(2,1)}, bf16[4,1,8,36,512]{4,3,2,1,0:T(8,128)(2,1)S(1)}) fusion(bf16[4,4,8,36,512]{4,3,2,1,0:T(8,128)(2,1)S(1)} %bitcast.90), kind=kLoop, calls=%fused_computation.54 | loop fusion | bytes 9437184 | tf_op jit(solution)/shard_map/slice | solution.py:64
  75.0 6.9 %bitcast_convert_fusion.4 = f32[4,4,8,36,512]{4,3,2,1,0:T(8,128)} fusion(bf16[16,128,1,512]{3,1,2,0:T(8,128)(2,1)S(1)} %copy-done, s32[16,8,128]{2,1,0:T(8,128)S(1)} %convolution_convert_fusion.2, pred[16,8,128]{2,1,0:T(8,128)(4,1)S(1)} %bitcast.96), kind=kOutput, calls=%fused_computation.51 | convolution fusion | flops 609878016 | bytes 11616256 | tf_op jit(solution)/shard_map/blct,btd->blcd/dot_general | solution.py:50
  81.9 39.2 %all-gather.4.cloned.1.call-done = bf16[8,4,4,36,768]{4,0,3,2,1:T(8,128)(2,1)} async-done(((bf16[8,1,4,36,768]{4,0,3,2,1:T(8,128)(2,1)}), bf16[8,4,4,36,768]{4,0,3,2,1:T(8,128)(2,1)}) %all-gather.4.cloned.1.call-update) | async-done | bytes 7077904 | tf_op jit(solution)/shard_map/all_gather | solution.py:35
  121.1 11.1 %fusion = f32[4,4,8,36]{3,0,1,2:T(4,128)S(1)} fusion(f32[4,4,8,36,512]{4,3,2,1,0:T(8,128)} %bitcast_convert_fusion.4, bf16[8,4,4,36,768]{4,0,3,2,1:T(8,128)(2,1)} %all-gather.4.cloned.1.call-done, bf16[8,768,512]{2,1,0:T(8,128)(2,1)} %param.9), kind=kOutput, calls=%fused_computation.8 | convolution fusion | flops 3628592640 | bytes 22824960 | tf_op jit(solution)/shard_map/liscf,lfd->silcd/dot_general | solution.py:71
  132.2 0.7 reshape.85
  132.9 4.7 %all-to-all-start.2 = ((f32[16,1,288]{2,1,0:T(1,128)}), f32[16,1,288]{2,1,0:T(1,128)S(1)}, u32[]{:S(2)}, u32[]{:S(2)}) async-start(f32[16,1,288]{2,1,0:T(1,128)} %reshape.85), calls=%async_computation.2 | async-start | bytes 49152 | tf_op jit(solution)/shard_map/all_to_all | solution.py:74
  137.7 3.6 %fusion.26 = (bf16[8,1,4,36,768]{4,0,3,2,1:T(8,128)(2,1)S(1)}, bf16[8,1,4,36,768]{4,0,3,2,1:T(8,128)(2,1)S(1)}, bf16[8,1,4,36,768]{4,0,3,2,1:T(8,128)(2,1)S(1)}, bf16[8,1,4,36,768]{4,0,3,2,1:T(8,128)(2,1)S(1)}) fusion(bf16[8,4,4,36,768]{4,0,3,2,1:T(8,128)(2,1)} %all-gather.4.cloned.1.call-done), kind=kLoop, calls=%fused_computation.53 | loop fusion | bytes 14155776 | tf_op jit(solution)/shard_map/slice | solution.py:63
  141.3 2.0 %fusion.12 = bf16[8,512,768,1]{2,1,3,0:T(8,128)(2,1)S(1)} fusion(bf16[8,1,4,36,768]{4,0,3,2,1:T(8,128)(2,1)S(1)} %get-tuple-element.15, bf16[4,1,8,36,512]{4,3,2,1,0:T(8,128)(2,1)S(1)} %copy-done.3), kind=kOutput, calls=%fused_computation.21 | convolution fusion | flops 905969664 | bytes 9240576 | tf_op jit(solution)/shard_map/lscf,slcd->lfd/dot_general | solution.py:61
  143.4 4.7 %fusion.13 = bf16[8,512,768,1]{2,1,3,0:T(8,128)(2,1)} fusion(bf16[8,1,4,36,768]{4,0,3,2,1:T(8,128)(2,1)S(1)} %get-tuple-element.16, bf16[4,1,8,36,512]{4,3,2,1,0:T(8,128)(2,1)S(1)} %copy-done.2), kind=kOutput, calls=%fused_computation.23 | convolution fusion | flops 905969664 | bytes 9240576 | tf_op jit(solution)/shard_map/lscf,slcd->lfd/dot_general | solution.py:61
  148.1 4.8 %fusion.14 = bf16[8,512,768,1]{2,1,3,0:T(8,128)(2,1)} fusion(bf16[8,1,4,36,768]{4,0,3,2,1:T(8,128)(2,1)S(1)} %get-tuple-element.17, bf16[4,1,8,36,512]{4,3,2,1,0:T(8,128)(2,1)S(1)} %get-tuple-element.21), kind=kOutput, calls=%fused_computation.25 | convolution fusion | flops 905969664 | bytes 9240576 | tf_op jit(solution)/shard_map/lscf,slcd->lfd/dot_general | solution.py:61
  152.8 9.2 %add_bitcast_fusion = f32[8,768,512]{1,2,0:T(8,128)} fusion(bf16[8,512,768,1]{2,1,3,0:T(8,128)(2,1)} %fusion.14, bf16[8,512,768,1]{2,1,3,0:T(8,128)(2,1)} %fusion.13, bf16[8,512,768,1]{2,1,3,0:T(8,128)(2,1)S(1)} %fusion.12, bf16[8,1,4,36,768]{4,0,3,2,1:T(8,128)(2,1)S(1)} %get-tuple-element.14, bf16[4,1,8,36,512]{4,3,2,1,0:T(8,128)(2,1)S(1)} %get-tuple-element.18), kind=kOutput, calls=%fused_computation.6 | convolution fusion | flops 931135488 | bytes 34406400 | tf_op jit(solution)/shard_map/lscf,slcd->lfd/dot_general | solution.py:61
  162.0 12.6 %copy.130 = f32[8,768,512]{2,1,0:T(8,128)} copy(f32[8,768,512]{1,2,0:T(8,128)} %add_bitcast_fusion) | data formatting | bytes 25165824
  174.6 0.5 broadcast.39
  175.1 0.7 reduce
  176.1 6.2 %gather_fusion = f32[1024]{0:T(1024)S(1)} fusion(f32[1152]{0:T(1024)S(1)} %reshape.52, s32[1024]{0:T(1024)S(1)} %broadcast_clamp_fusion), kind=kCustom, calls=%fused_computation | custom fusion | bytes 12288 | tf_op jit(solution)/shard_map/gather | solution.py:84
  182.3 0.7 copy.131
  (33 shorter events, 0.8 us)
Async XLA Ops:
  7.2 15.5 %copy-start.1 = (bf16[8,1,4,36,768]{4,2,3,1,0:T(4,128)(2,1)S(1)}, bf16[8,1,4,36,768]{4,2,3,1,0:T(4,128)(2,1)}, u32[]{:S(2)}) copy-start(bf16[8,1,4,36,768]{4,2,3,1,0:T(4,128)(2,1)} %param.8) | copy-start | bytes 5308420
  7.2 62.6 %all-gather.6.cloned.1.call-start = ((), (), s32[]{:S(2)}) async-start(), calls=%async_computation.4 | async-start | bytes 2621440 | tf_op jit(solution)/shard_map/all_gather | solution.py:24
  22.6 1.9 copy-start.5
  22.6 7.5 %copy-start.4 = (s32[128,8]{0,1:T(8,128)S(1)}, s32[128,8]{0,1:T(8,128)}, u32[]{:S(2)}) copy-start(s32[128,8]{0,1:T(8,128)} %param.7) | copy-start | bytes 12292
  22.6 98.5 %all-gather.4.cloned.1.call-start = ((), (), s32[]{:S(2)}) async-start(), calls=%async_computation.3 | async-start | bytes 8847360 | tf_op jit(solution)/shard_map/all_gather | solution.py:35
  25.1 35.6 %all-to-all-start = ((bf16[16,128,8]{1,2,0:T(8,128)(2,1)}), bf16[16,128,8]{1,2,0:T(8,128)(2,1)S(1)}, u32[]{:S(2)}, u32[]{:S(2)}) async-start(bf16[16,128,8]{1,2,0:T(8,128)(2,1)} %stack.2), calls=%async_computation | async-start | bytes 65536 | tf_op jit(solution)/shard_map/all_to_all | solution.py:29
  72.9 2.0 %copy-start = (bf16[16,128,1,512]{3,1,2,0:T(8,128)(2,1)S(1)}, bf16[16,128,1,512]{3,1,2,0:T(8,128)(2,1)}, u32[]{:S(2)}) copy-start(bf16[16,128,1,512]{3,1,2,0:T(8,128)(2,1)} %all-gather.6.cloned.1.call-done) | copy-start | bytes 6291460
  132.9 41.7 %all-to-all-start.2 = ((f32[16,1,288]{2,1,0:T(1,128)}), f32[16,1,288]{2,1,0:T(1,128)S(1)}, u32[]{:S(2)}, u32[]{:S(2)}) async-start(f32[16,1,288]{2,1,0:T(1,128)} %reshape.85), calls=%async_computation.2 | async-start | bytes 49152 | tf_op jit(solution)/shard_map/all_to_all | solution.py:74
  137.7 3.6 %copy-start.3 = (bf16[4,1,8,36,512]{4,3,2,1,0:T(8,128)(2,1)S(1)}, bf16[4,1,8,36,512]{4,3,2,1,0:T(8,128)(2,1)}, u32[]{:S(2)}) copy-start(bf16[4,1,8,36,512]{4,3,2,1,0:T(8,128)(2,1)} %get-tuple-element.19) | copy-start | bytes 3538948
  141.3 2.1 %copy-start.2 = (bf16[4,1,8,36,512]{4,3,2,1,0:T(8,128)(2,1)S(1)}, bf16[4,1,8,36,512]{4,3,2,1,0:T(8,128)(2,1)}, u32[]{:S(2)}) copy-start(bf16[4,1,8,36,512]{4,3,2,1,0:T(8,128)(2,1)} %get-tuple-element.20) | copy-start | bytes 3538948
Sparse Core Ops, SparseCore 0:
  22.7 47.0 all-gather.5
  71.4 49.6 all-gather.3
